TPU v7x, 512 devices: a whole 4x4x16 slice. The times are simulated.
512 devices in a mesh: fsdp: 128 (over z, y, core), seq: 4 (over x).
Axes of the slice: x: 4, y: 4, z: 16, core: 2. Of those that a mesh axis runs over, the one named last changes fastest.
Arguments:
- tokens: bfloat16 [128, 512, 8192], P('fsdp', 'seq'), may hold values from -6 to 6
- queries: bfloat16 [128, 512, 8192], P('fsdp', None, 'seq'), may hold values from -6 to 6
- key_weight: bfloat16 [8192, 1024], P('fsdp', 'seq'), may hold values from -1 to 1
- u_factor: float32 [8192, 64], P('fsdp'), may hold values from -6 to 6
- v_factor: float32 [1024, 64], replicated, may hold values from -6 to 6
Outputs:
- update: float32 [8192, 1024], P('fsdp')
- losses: float32 [2], replicated
All inputs are finite; a program needn't handle non-finite values.
Results may differ from a plain program's by a relative error of at most 0.0003.
Values may be sent and summed in bfloat16 or wider, within the bound.
No kernel may reach another device: no remote copies, remote signals or barrier semaphores. Data moves between devices by JAX's collectives and lax.ppermute only.
A program may use at most 64 MiB of HBM per device.

v0:
```python
import math
import jax
import jax.numpy as jnp
from jax import lax
from jax.sharding import PartitionSpec as P

D = 8192
HQ = 64
HD = 128
R = 64
KD = 1024
GROUP = 8


def highest(left, right):
    return jnp.dot(left, right, precision=lax.Precision.HIGHEST, preferred_element_type=jnp.float32)


def solve_rows(rows, gram):
    lower = jnp.linalg.cholesky(gram)
    return lax.linalg.triangular_solve(lower, rows, left_side=False, lower=True, transpose_a=True)


def local(tokens, queries, key_weight, u_factor, v_factor):
    q_v = v_factor
    for turn in range(2):
        q_v = solve_rows(q_v, highest(q_v.T, q_v))
    u_rows = u_factor
    for turn in range(2):
        whole_u = lax.all_gather(u_rows, "fsdp", axis=0, tiled=True)
        u_rows = solve_rows(u_rows, highest(whole_u.T, whole_u))
    q_low = u_rows.astype(jnp.bfloat16)
    whole_x = lax.all_gather(tokens, "seq", axis=1, tiled=True)[0]
    length = whole_x.shape[0]
    slice_width = key_weight.shape[1]
    weight_piece = lax.all_gather(key_weight, "fsdp", axis=0, tiled=True)
    factor_piece = lax.all_gather(q_low, "fsdp", axis=0, tiled=True)
    base = jnp.dot(whole_x, weight_piece, preferred_element_type=jnp.float32)
    side = jnp.dot(whole_x, factor_piece, preferred_element_type=jnp.float32)
    col_start = lax.axis_index("seq") * slice_width
    v_slice = lax.dynamic_slice_in_dim(q_v, col_start, slice_width, 0)
    offset = 2.0 * highest(side, v_slice.T)
    keys = jnp.stack([base + offset, base - offset]).astype(jnp.bfloat16)
    local_kv = slice_width // HD
    query_rows = queries[0]
    query_heads = query_rows.reshape(length, local_kv, GROUP, HD).transpose(1, 2, 0, 3)
    key_heads = keys.reshape(2, length, local_kv, HD).transpose(2, 0, 1, 3)
    places = jnp.arange(length)
    causal = places[:, None] >= places[None, :]
    factor_scale = 1.0 / math.sqrt(HD)

    def one_query_head(query_one, key_one):
        scores = (
            jnp.einsum("td,npd->ntp", query_one, key_one, preferred_element_type=jnp.float32)
            * factor_scale
        )
        scores = jnp.where(causal[None], scores, -1e30)
        top = jnp.max(scores, axis=-1)
        total = jnp.sum(jnp.where(causal[None], jnp.exp(scores - top[..., None]), 0.0), axis=-1)
        return jnp.sum(top + jnp.log(total), axis=1)

    def one_key_head(pair):
        group_queries, key_one = pair
        return jnp.sum(
            lax.map(lambda query_one: one_query_head(query_one, key_one), group_queries), axis=0
        )

    partial_sums = jnp.sum(lax.map(one_key_head, (query_heads, key_heads)), axis=0)
    sums = lax.psum(partial_sums, ("fsdp", "seq"))
    losses = sums / (lax.axis_size("fsdp") * length * HQ)
    unit = math.sqrt(D * KD / R)
    update = unit * highest(u_rows, q_v.T)
    return (update, losses)


def solution(mesh):
    in_specs = (
        P("fsdp", "seq", None),
        P("fsdp", None, "seq"),
        P("fsdp", "seq"),
        P("fsdp", None),
        P(),
    )
    out_specs = (P("fsdp", None), P())
    return jax.shard_map(local, mesh=mesh, in_specs=in_specs, out_specs=out_specs, check_vma=False)
```

profile of v0, /device:TPU:1, one launch (start us, length us, event | category | flops | bytes accessed | tf_op | source)
XLA Modules:
  0.0 858.6 jit_solution(16340279235827252313)
XLA Ops:
  8.0 151.0 %all-gather.6.cloned.1.call-done = f32[8192,64]{1,0:T(8,128)} async-done(((f32[64,64]{1,0:T(8,128)}), f32[8192,64]{1,0:T(8,128)}) %all-gather.6.cloned.1.call-update) | async-done | bytes 2097168 | tf_op jit(solution)/shard_map/all_gather | solution.py:30
  159.0 10.4 %fusion.30 = f32[64,64]{1,0:T(8,128)S(1)} fusion(f32[8192,64]{1,0:T(8,128)} %all-gather.6.cloned.1.call-done), kind=kOutput, calls=%fused_computation.63 | convolution fusion | flops 402653184 | bytes 2113536 | tf_op jit(solution)/shard_map/dot_general | solution.py:16
  169.5 5.8 cholesky.74
  176.7 4.9 custom-call.10
  182.8 137.7 %all-gather.8.cloned.1.call-done = f32[8192,64]{1,0:T(8,128)} async-done(((f32[64,64]{1,0:T(8,128)}), f32[8192,64]{1,0:T(8,128)}) %all-gather.8.cloned.1.call-update) | async-done | bytes 2097168 | tf_op jit(solution)/shard_map/all_gather | solution.py:30
  320.6 10.4 %fusion.31 = f32[64,64]{1,0:T(8,128)S(1)} fusion(f32[8192,64]{1,0:T(8,128)} %all-gather.8.cloned.1.call-done), kind=kOutput, calls=%fused_computation.64 | convolution fusion | flops 402653184 | bytes 2113536 | tf_op jit(solution)/shard_map/dot_general | solution.py:16
  331.1 5.8 cholesky.85
  338.3 4.9 custom-call.11
  345.8 5.8 cholesky.96
  353.0 4.9 custom-call.12
  358.8 5.9 cholesky.107
  366.0 4.9 custom-call.13
  370.9 2.8 copy.26
  374.1 107.1 %all-gather.14.cloned.1.call-done = bf16[8192,64]{1,0:T(8,128)(2,1)} async-done(((bf16[64,64]{1,0:T(8,128)(2,1)}), bf16[8192,64]{1,0:T(8,128)(2,1)}) %all-gather.14.cloned.1.call-update) | async-done | bytes 1048592 | tf_op jit(solution)/shard_map/all_gather | solution.py:37
  481.1 88.4 %all-gather.10.cloned.1.call-done = bf16[1,512,8192]{2,1,0:T(8,128)(2,1)} async-done(((bf16[1,128,8192]{2,1,0:T(8,128)(2,1)}), bf16[1,512,8192]{2,1,0:T(8,128)(2,1)}) %all-gather.10.cloned.1.call-update) | async-done | bytes 8388624 | tf_op jit(solution)/shard_map/all_gather | solution.py:33
  569.6 6.7 fusion.9
  576.9 139.4 %all-gather.12.cloned.1.call-done = bf16[8192,256]{1,0:T(8,128)(2,1)} async-done(((bf16[64,256]{1,0:T(8,128)(2,1)}), bf16[8192,256]{1,0:T(8,128)(2,1)}) %all-gather.12.cloned.1.call-update) | async-done | bytes 4194320 | tf_op jit(solution)/shard_map/all_gather | solution.py:36
  716.3 6.9 add_convert_fusion
  723.7 25.3 %while.26 = (s32[]{:T(128)}, f32[2,2]{1,0:T(2,128)S(1)}, bf16[2,8,512,128]{2,3,1,0:T(8,128)(2,1)}, bf16[2,2,512,128]{3,2,1,0:T(8,128)(2,1)S(1)}, s32[]{:T(128)},...) while((s32[]{:T(128)}, f32[2,2]{1,0:T(2,128)S(1)}, ...), condition=%wide.region_9.13_spmd.clone.clone, body=%wide.region_2.12_spmd.clone.clone.sunk | while | flops 138674192 | bytes 10113394 | solution.py:68
  723.7 1.3 constant_dynamic-slice_fusion.2
  725.8 10.4 %while.27 = (s32[]{:T(128)}, f32[8,2]{1,0:T(8,128)S(1)}, pred[512,512]{0,1:T(8,128)(4,1)S(1)}, bf16[8,512,128]{2,1,0:T(8,128)(2,1)S(1)}, bf16[2,512,128]{2,1,0:T(8,128)(2,1)S(1)}, /*index=5*/s32[]{:T(128)}, s32[]{:T(128)}) while((s32[]{:T(128)}, f32[8,2]{1,0:T(8,128)S(1)}, pred[512,512]{0,1:T(8,128)(4,1)S(1)}, ...), condition=%wide.region_7.10_spmd.clone, body=%wide.region_3.9_spmd.clone.sunk | while | flops 138412032 | bytes 5132397 | solution.py:65
  736.3 1.3 constant_dynamic-slice_fusion.2
  738.5 10.4 %while.27 = (s32[]{:T(128)}, f32[8,2]{1,0:T(8,128)S(1)}, pred[512,512]{0,1:T(8,128)(4,1)S(1)}, bf16[8,512,128]{2,1,0:T(8,128)(2,1)S(1)}, bf16[2,512,128]{2,1,0:T(8,128)(2,1)S(1)}, /*index=5*/s32[]{:T(128)}, s32[]{:T(128)}) while((s32[]{:T(128)}, f32[8,2]{1,0:T(8,128)S(1)}, pred[512,512]{0,1:T(8,128)(4,1)S(1)}, ...), condition=%wide.region_7.10_spmd.clone, body=%wide.region_3.9_spmd.clone.sunk | while | flops 138412032 | bytes 5132397 | solution.py:65
  750.1 101.5 %psum.7 = f32[2]{0:T(128)S(1)} all-reduce(f32[2]{0:T(128)S(1)} %reduce_sum.36), channel_id=1, replica_groups=mesh['fsdp'=128,'seq'=4] {'fsdp','seq'}, use_global_device_ids=true, to_apply=%region_11.15 | all-reduce | flops 2 | bytes 16 | tf_op jit(solution)/shard_map/psum | solution.py:69
  (128 shorter events, 36.2 us)
Async XLA Ops:
  7.2 338.2 %copy-start = (f32[1024,64]{0,1:T(8,128)S(1)}, f32[1024,64]{0,1:T(8,128)}, u32[]{:S(2)}) copy-start(f32[1024,64]{0,1:T(8,128)} %param.18) | copy-start | bytes 786436
  7.2 151.8 %all-gather.6.cloned.1.call-start = ((), (), s32[]{:S(2)}) async-start(), calls=%async_computation | async-start | bytes 4227072 | tf_op jit(solution)/shard_map/all_gather | solution.py:30
  7.9 173.7 %copy-start.2 = (f32[64,64]{1,0:T(8,128)S(1)}, f32[64,64]{1,0:T(8,128)}, u32[]{:S(2)}) copy-start(f32[64,64]{1,0:T(8,128)} %param.17) | copy-start | bytes 49156
  7.9 312.6 %all-gather.8.cloned.1.call-start = ((), (), s32[]{:S(2)}) async-start(), calls=%async_computation.1 | async-start | bytes 4227072 | tf_op jit(solution)/shard_map/all_gather | solution.py:30
  182.6 298.5 %all-gather.14.cloned.1.call-start = ((), (), s32[]{:S(2)}) async-start(), calls=%async_computation.4 | async-start | bytes 2113536 | tf_op jit(solution)/shard_map/all_gather | solution.py:37
  344.2 26.7 %copy-start.1 = (bf16[1,512,2048]{2,1,0:T(8,128)(2,1)S(1)}, bf16[1,512,2048]{2,1,0:T(8,128)(2,1)}, u32[]{:S(2)}) copy-start(bf16[1,512,2048]{2,1,0:T(8,128)(2,1)} %param.15) | copy-start | bytes 6291460
  344.2 225.4 %all-gather.10.cloned.1.call-start = ((), (), s32[]{:S(2)}) async-start(), calls=%async_computation.2 | async-start | bytes 10485760 | tf_op jit(solution)/shard_map/all_gather | solution.py:33
  344.7 371.6 %all-gather.12.cloned.1.call-start = ((), (), s32[]{:S(2)}) async-start(), calls=%async_computation.3 | async-start | bytes 4227072 | tf_op jit(solution)/shard_map/all_gather | solution.py:36
Sparse Core Ops, SparseCore 0:
  11.1 147.8 all-gather.5
  182.7 137.7 all-gather.7
  344.3 136.8 all-gather.13
  483.1 86.4 all-gather.9
  572.5 143.6 all-gather.11
where the time goes:
time: 859 us
  waiting for transfers between devices  625 us (73%)
  blocking collectives  101 us (12%)
  other arithmetic  60.3 us (7%)
  matrix products  47.2 us (5%)
  between operations  14 us (2%)
  local copies, waits for them, and re-layouts  9.49 us (1%)
    all_gather x2, waiting for transfers between devices, local(): whole_u = lax.all_gather(u_rows, 'fsdp', axis=0, tiled=True)  289 us
    all_gather x1, waiting for transfers between devices, local(): weight_piece = lax.all_gather(key_weight, 'fsdp', axis=0, tiled=True)  139 us
    all_gather x1, waiting for transfers between devices, local(): factor_piece = lax.all_gather(q_low, 'fsdp', axis=0, tiled=True)  107 us
    psum x1, blocking collectives, local(): sums = lax.psum(partial_sums, ('fsdp', 'seq'))  101 us
    all_gather x1, waiting for transfers between devices, local(): whole_x = lax.all_gather(tokens, 'seq', axis=1, tiled=True)[0]  88.4 us
    another operation x12, other arithmetic, solve_rows(): lower = jnp.linalg.cholesky(gram)  26.1 us
    dot_general x6, matrix products, highest(): jnp.dot(left, right, precision=lax.Precision.HIGHEST, preferred_element_t...  23.4 us
    another operation x8, other arithmetic, solve_rows(): lax.linalg.triangular_solve(lower, rows, left_side=False, lower=True, tra...  22.2 us
  transfers between devices with their start and end apart: 5, of which 5 were waited for; matrix products, arithmetic and copies ran while one was open for 4% of the time, Pallas kernels for 0%

commit v1 on v0

--- a/solution.py
+++ b/solution.py
@@ -30,7 +30,10 @@
         whole_u = lax.all_gather(u_rows, "fsdp", axis=0, tiled=True)
         u_rows = solve_rows(u_rows, highest(whole_u.T, whole_u))
     q_low = u_rows.astype(jnp.bfloat16)
-    whole_x = lax.all_gather(tokens, "seq", axis=1, tiled=True)[0]
+    attach_view = lambda state: jnp.concatenate(
+        lax.all_to_all(jnp.stack(lax.axis_size("seq") * [state], 0), "seq", 0, 0), 1
+    )
+    whole_x = attach_view(tokens)[0]
     length = whole_x.shape[0]
     slice_width = key_weight.shape[1]
     weight_piece = lax.all_gather(key_weight, "fsdp", axis=0, tiled=True)

time: 859 us -> 765 us (0.89)
  waiting for transfers between devices: 625 us -> 521 us
    all_gather x1 -> x0, waiting for transfers between devices: 88.4 us -> none  [local(): whole_x = lax.all_gather(tokens, 'seq', axis=1, tiled=True)[0]]
    all_gather x1, waiting for transfers between devices: 107 us -> 32.4 us  [local(): factor_piece = lax.all_gather(q_low, 'fsdp', axis=0, tiled=True)]
    all_to_all x0 -> x1, waiting for transfers between devices: none -> 64.9 us  [local(): lax.all_to_all(jnp.stack(lax.axis_size('seq') * [state], 0), 'seq', 0, 0)]
  transfers between devices with their start and end apart: 5 -> 5, of which waited for: 5 -> 5; matrix products, arithmetic and copies ran while one was open for 4% -> 5% of each run, Pallas kernels for 0% -> 0%
where the time goes in v1:
time: 765 us
  waiting for transfers between devices  521 us (68%)
  blocking collectives  101 us (13%)
  other arithmetic  60.2 us (8%)
  matrix products  47.1 us (6%)
  between operations  14 us (2%)
  local copies, waits for them, and re-layouts  13.6 us (2%)
    all_gather x2, waiting for transfers between devices, local(): whole_u = lax.all_gather(u_rows, 'fsdp', axis=0, tiled=True)  289 us
    all_gather x1, waiting for transfers between devices, local(): weight_piece = lax.all_gather(key_weight, 'fsdp', axis=0, tiled=True)  134 us
    psum x1, blocking collectives, local(): sums = lax.psum(partial_sums, ('fsdp', 'seq'))  101 us
    all_to_all x1, waiting for transfers between devices, local(): lax.all_to_all(jnp.stack(lax.axis_size('seq') * [state], 0), 'seq', 0, 0)  64.9 us
    all_gather x1, waiting for transfers between devices, local(): factor_piece = lax.all_gather(q_low, 'fsdp', axis=0, tiled=True)  32.4 us
    another operation x12, other arithmetic, solve_rows(): lower = jnp.linalg.cholesky(gram)  26.1 us
    dot_general x6, matrix products, highest(): jnp.dot(left, right, precision=lax.Precision.HIGHEST, preferred_element_t...  23.3 us
    another operation x8, other arithmetic, solve_rows(): lax.linalg.triangular_solve(lower, rows, left_side=False, lower=True, tra...  22.2 us
  transfers between devices with their start and end apart: 5, of which 5 were waited for; matrix products, arithmetic and copies ran while one was open for 5% of the time, Pallas kernels for 0%

profile of v1, /device:TPU:1, one launch (start us, length us, event | category | flops | bytes accessed | tf_op | source)
XLA Modules:
  0.0 764.6 jit_solution(9688253466576569146)
XLA Ops:
  8.0 151.0 %all-gather.5.cloned.1.call-done = f32[8192,64]{1,0:T(8,128)} async-done(((f32[64,64]{1,0:T(8,128)}), f32[8192,64]{1,0:T(8,128)}) %all-gather.5.cloned.1.call-update) | async-done | bytes 2097168 | tf_op jit(solution)/shard_map/all_gather | solution.py:30
  159.0 10.4 %fusion.26 = f32[64,64]{1,0:T(8,128)S(1)} fusion(f32[8192,64]{1,0:T(8,128)} %all-gather.5.cloned.1.call-done), kind=kOutput, calls=%fused_computation.59 | convolution fusion | flops 402653184 | bytes 2113536 | tf_op jit(solution)/shard_map/dot_general | solution.py:16
  169.5 5.8 cholesky.74
  176.7 4.9 custom-call.10
  182.8 137.7 %all-gather.7.cloned.1.call-done = f32[8192,64]{1,0:T(8,128)} async-done(((f32[64,64]{1,0:T(8,128)}), f32[8192,64]{1,0:T(8,128)}) %all-gather.7.cloned.1.call-update) | async-done | bytes 2097168 | tf_op jit(solution)/shard_map/all_gather | solution.py:30
  320.6 10.4 %fusion.27 = f32[64,64]{1,0:T(8,128)S(1)} fusion(f32[8192,64]{1,0:T(8,128)} %all-gather.7.cloned.1.call-done), kind=kOutput, calls=%fused_computation.60 | convolution fusion | flops 402653184 | bytes 2113536 | tf_op jit(solution)/shard_map/dot_general | solution.py:16
  331.1 5.8 cholesky.85
  338.3 4.9 custom-call.11
  344.7 4.4 stack.16
  349.2 6.0 all-to-all-start
  355.7 5.8 cholesky.96
  362.8 4.9 custom-call.12
  368.6 5.8 cholesky.107
  375.8 4.9 custom-call.13
  380.7 2.5 copy.26
  383.7 64.9 %all-to-all-done = bf16[4,1,128,8192]{3,2,1,0:T(8,128)(2,1)} async-done(((bf16[4,1,128,8192]{3,2,1,0:T(8,128)(2,1)}), bf16[4,1,128,8192]{3,2,1,0:T(8,128)(2,1)}, u32[]{:S(2)}, u32[]{:S(2)}) %all-to-all-start) | async-done | bytes 8388640 | tf_op jit(solution)/shard_map/all_to_all | solution.py:34
  448.6 32.4 %all-gather.11.cloned.1.call-done = bf16[8192,64]{1,0:T(8,128)(2,1)} async-done(((bf16[64,64]{1,0:T(8,128)(2,1)}), bf16[8192,64]{1,0:T(8,128)(2,1)}) %all-gather.11.cloned.1.call-update) | async-done | bytes 1048592 | tf_op jit(solution)/shard_map/all_gather | solution.py:40
  481.0 6.7 fusion.30
  488.3 134.1 %all-gather.9.cloned.1.call-done = bf16[8192,256]{1,0:T(8,128)(2,1)} async-done(((bf16[64,256]{1,0:T(8,128)(2,1)}), bf16[8192,256]{1,0:T(8,128)(2,1)}) %all-gather.9.cloned.1.call-update) | async-done | bytes 4194320 | tf_op jit(solution)/shard_map/all_gather | solution.py:39
  622.4 6.9 add_convert_fusion
  629.8 25.2 %while.26 = (s32[]{:T(128)}, f32[2,2]{1,0:T(2,128)S(1)}, bf16[2,8,512,128]{2,3,1,0:T(8,128)(2,1)}, bf16[2,2,512,128]{3,2,1,0:T(8,128)(2,1)S(1)}, s32[]{:T(128)},...) while((s32[]{:T(128)}, f32[2,2]{1,0:T(2,128)S(1)}, ...), condition=%wide.region_9.13_spmd.clone.clone, body=%wide.region_2.12_spmd.clone.clone.sunk | while | flops 138674192 | bytes 10113394 | solution.py:71
  631.9 10.4 %while.27 = (s32[]{:T(128)}, f32[8,2]{1,0:T(8,128)S(1)}, pred[512,512]{0,1:T(8,128)(4,1)S(1)}, bf16[8,512,128]{2,1,0:T(8,128)(2,1)S(1)}, bf16[2,512,128]{2,1,0:T(8,128)(2,1)S(1)}, /*index=5*/s32[]{:T(128)}, s32[]{:T(128)}) while((s32[]{:T(128)}, f32[8,2]{1,0:T(8,128)S(1)}, pred[512,512]{0,1:T(8,128)(4,1)S(1)}, ...), condition=%wide.region_7.10_spmd.clone, body=%wide.region_3.9_spmd.clone.sunk | while | flops 138412032 | bytes 5132397 | solution.py:68
  644.5 10.4 %while.27 = (s32[]{:T(128)}, f32[8,2]{1,0:T(8,128)S(1)}, pred[512,512]{0,1:T(8,128)(4,1)S(1)}, bf16[8,512,128]{2,1,0:T(8,128)(2,1)S(1)}, bf16[2,512,128]{2,1,0:T(8,128)(2,1)S(1)}, /*index=5*/s32[]{:T(128)}, s32[]{:T(128)}) while((s32[]{:T(128)}, f32[8,2]{1,0:T(8,128)S(1)}, pred[512,512]{0,1:T(8,128)(4,1)S(1)}, ...), condition=%wide.region_7.10_spmd.clone, body=%wide.region_3.9_spmd.clone.sunk | while | flops 138412032 | bytes 5132397 | solution.py:68
  656.1 101.5 %psum.7 = f32[2]{0:T(128)S(1)} all-reduce(f32[2]{0:T(128)S(1)} %reduce_sum.36), channel_id=1, replica_groups=mesh['fsdp'=128,'seq'=4] {'fsdp','seq'}, use_global_device_ids=true, to_apply=%region_11.15 | all-reduce | flops 2 | bytes 16 | tf_op jit(solution)/shard_map/psum | solution.py:72
  (130 shorter events, 38.1 us)
Async XLA Ops:
  7.2 348.0 %copy-start = (f32[1024,64]{0,1:T(8,128)S(1)}, f32[1024,64]{0,1:T(8,128)}, u32[]{:S(2)}) copy-start(f32[1024,64]{0,1:T(8,128)} %param.18) | copy-start | bytes 786436
  7.2 151.8 %all-gather.5.cloned.1.call-start = ((), (), s32[]{:S(2)}) async-start(), calls=%async_computation.1 | async-start | bytes 4227072 | tf_op jit(solution)/shard_map/all_gather | solution.py:30
  7.9 173.7 %copy-start.3 = (f32[64,64]{1,0:T(8,128)S(1)}, f32[64,64]{1,0:T(8,128)}, u32[]{:S(2)}) copy-start(f32[64,64]{1,0:T(8,128)} %param.17) | copy-start | bytes 49156
  7.9 312.6 %all-gather.7.cloned.1.call-start = ((), (), s32[]{:S(2)}) async-start(), calls=%async_computation.2 | async-start | bytes 4227072 | tf_op jit(solution)/shard_map/all_gather | solution.py:30
  182.6 162.1 %copy-start.1 = (bf16[1,128,8192]{2,1,0:T(8,128)(2,1)S(1)}, bf16[1,128,8192]{2,1,0:T(8,128)(2,1)}, u32[]{:S(2)}) copy-start(bf16[1,128,8192]{2,1,0:T(8,128)(2,1)} %param.14) | copy-start | bytes 6291460
  182.6 298.4 %all-gather.11.cloned.1.call-start = ((), (), s32[]{:S(2)}) async-start(), calls=%async_computation.4 | async-start | bytes 2113536 | tf_op jit(solution)/shard_map/all_gather | solution.py:40
  344.2 278.2 %all-gather.9.cloned.1.call-start = ((), (), s32[]{:S(2)}) async-start(), calls=%async_computation.3 | async-start | bytes 4227072 | tf_op jit(solution)/shard_map/all_gather | solution.py:39
  349.2 31.6 %copy-start.2 = (bf16[1,512,2048]{2,1,0:T(8,128)(2,1)S(1)}, bf16[1,512,2048]{2,1,0:T(8,128)(2,1)}, u32[]{:S(2)}) copy-start(bf16[1,512,2048]{2,1,0:T(8,128)(2,1)} %param.15) | copy-start | bytes 6291460
  349.2 99.4 %all-to-all-start = ((bf16[4,1,128,8192]{3,2,1,0:T(8,128)(2,1)}), bf16[4,1,128,8192]{3,2,1,0:T(8,128)(2,1)}, u32[]{:S(2)}, u32[]{:S(2)}) async-start(bf16[4,1,128,8192]{3,2,1,0:T(8,128)(2,1)} %stack.16), calls=%async_computation | async-start | bytes 16777216 | tf_op jit(solution)/shard_map/all_to_all | solution.py:34
Sparse Core Ops, SparseCore 0:
  11.1 147.8 all-gather.4
  182.7 137.7 all-gather.6
  344.3 136.6 all-gather.10
  484.0 138.3 all-gather.8
